TPU v7x, 256 devices: a whole 4x4x8 slice. The times are simulated.
256 devices in a mesh: dp: 32 (over z, x), et: 8 (over y, core).
Axes of the slice: x: 4, y: 4, z: 8, core: 2. Of those that a mesh axis runs over, the one named last changes fastest.
Arguments:
- tokens: bfloat16 [4096, 2048], P('dp', 'et'), may hold values from -6 to 6
- cotangent: bfloat16 [4096, 2048], P('dp', 'et'), may hold values from -1.5 to 1.5
- expert_ids: int32 [4096, 8], P('dp'), may hold values from 0 to 63, all different within a row; in each aligned block of 128 rows (0 to 127, 128 to 255, ...) at most 24 rows name the same one
- route_gates: bfloat16 [4096, 8], P('dp'), may hold values from 0.049804688 to 0.3984375
- gate_proj: bfloat16 [64, 2048, 1024], P('dp', None, 'et'), may hold values from -0.125 to 0.125
- up_proj: bfloat16 [64, 2048, 1024], P('dp', None, 'et'), may hold values from -0.125 to 0.125
- down_proj: bfloat16 [64, 1024, 2048], P('dp', 'et'), may hold values from -0.1875 to 0.1875
Outputs:
- mixed: bfloat16 [4096, 2048], P('dp', 'et')
- grad_tokens: bfloat16 [4096, 2048], P('dp', 'et')
- grad_gates: float32 [4096, 8], P('dp')
- grad_gate_proj: float32 [64, 2048, 1024], P('dp', None, 'et')
- grad_up_proj: float32 [64, 2048, 1024], P('dp', None, 'et')
- grad_down_proj: float32 [64, 1024, 2048], P('dp', 'et')
Inputs may be any that keep to these rules, and one draw needn't show every extreme that they name: `expert_ids`: each row names 8 different experts. Among the rows of one device (128 aligned rows), no expert is named more than 24 times, a bound that some block reaches.
All inputs are finite; a program needn't handle non-finite values.
Results may differ from a plain program's by a relative error of at most 0.015.
Values may be sent and summed in bfloat16 or wider, within the bound.
No kernel may reach another device: no remote copies, remote signals or barrier semaphores. Data moves between devices by JAX's collectives and lax.ppermute only.
A program may use at most 128 MiB of HBM per device.

v0:
```python
import jax
import jax.numpy as jnp
from jax import lax
from jax.sharding import PartitionSpec as P


def places_in_block(chosen, experts):
    flattened = chosen.reshape(-1)
    pairs = flattened.shape[0]
    onehot = (flattened[:, None] == jnp.arange(experts, dtype=jnp.int32)[None, :]).astype(
        jnp.bfloat16
    )
    rows = lax.broadcasted_iota(jnp.int32, (pairs, pairs), 0)
    cols = lax.broadcasted_iota(jnp.int32, (pairs, pairs), 1)
    earlier = (cols < rows).astype(jnp.bfloat16)
    before = jnp.dot(earlier, onehot, preferred_element_type=jnp.float32)
    return jnp.sum(before * onehot.astype(jnp.float32), axis=1).astype(jnp.int32)


def local(tokens, cotangent, expert_ids, route_gates, gate_proj, up_proj, down_proj):
    groups = lax.axis_size("dp")
    shards = lax.axis_size("et")
    local_experts, features, units = gate_proj.shape
    experts = local_experts * groups
    tok_rows, per_token = expert_ids.shape
    width = tokens.shape[1]
    capacity = 3 * tok_rows * per_token // (2 * experts)
    slots = experts * capacity
    places = places_in_block(expert_ids, experts)
    slot_index = (expert_ids.reshape(-1) * capacity + places).reshape(tok_rows, per_token)
    pairs = tok_rows * per_token
    pair_slot = (
        slot_index.reshape(pairs, 1) == jnp.arange(slots, dtype=jnp.int32)[None, :]
    ).astype(jnp.bfloat16)
    owner = lax.broadcasted_iota(
        jnp.int32, (tok_rows, pairs), 1
    ) // per_token == lax.broadcasted_iota(jnp.int32, (tok_rows, pairs), 0)
    gate_owner = jnp.where(owner, route_gates.reshape(1, pairs), jnp.zeros((), jnp.bfloat16))
    select = jnp.einsum(
        "tp,ps->st", owner.astype(jnp.bfloat16), pair_slot, preferred_element_type=jnp.float32
    ).astype(jnp.bfloat16)
    gate_select = jnp.einsum(
        "tp,ps->st", gate_owner, pair_slot, preferred_element_type=jnp.float32
    ).astype(jnp.bfloat16)
    picked = jnp.dot(select, tokens, preferred_element_type=jnp.float32).astype(jnp.bfloat16)
    scaled = jnp.dot(gate_select, cotangent, preferred_element_type=jnp.float32).astype(
        jnp.bfloat16
    )
    expert_in_part, expert_cot_part = (
        lax.all_to_all(
            picked.reshape(experts, capacity, width), "dp", split_axis=0, concat_axis=1, tiled=True
        ),
        lax.all_to_all(
            scaled.reshape(experts, capacity, width), "dp", split_axis=0, concat_axis=1, tiled=True
        ),
    )
    expert_in = lax.all_gather(expert_in_part, "et", axis=0)
    expert_cot = lax.all_gather(expert_cot_part, "et", axis=0)
    gate_w = gate_proj.reshape(local_experts, shards, width, units)
    up_w = up_proj.reshape(local_experts, shards, width, units)
    down_w = down_proj.reshape(local_experts, units, shards, width)
    pre_gate = jnp.einsum("jesd,ejdf->esf", expert_in, gate_w, preferred_element_type=jnp.float32)
    pre_up = jnp.einsum("jesd,ejdf->esf", expert_in, up_w, preferred_element_type=jnp.float32)
    sigmoid_gate = jax.nn.sigmoid(pre_gate)
    silu_gate = pre_gate * sigmoid_gate
    hidden = (silu_gate * pre_up).astype(jnp.bfloat16)
    out_part = jnp.einsum("esf,efd->esd", hidden, down_proj, preferred_element_type=jnp.float32)
    grad_hidden = jnp.einsum(
        "jesd,efjd->esf", expert_cot, down_w, preferred_element_type=jnp.float32
    )
    grad_pre_gate = (
        grad_hidden * pre_up * sigmoid_gate * (1.0 + pre_gate * (1.0 - sigmoid_gate))
    ).astype(jnp.bfloat16)
    grad_pre_up = (grad_hidden * silu_gate).astype(jnp.bfloat16)
    grad_down = jnp.einsum(
        "esf,jesd->efjd", hidden, expert_cot, preferred_element_type=jnp.float32
    ).reshape(local_experts, units, features)
    grad_gate_w = jnp.einsum(
        "jesd,esf->ejdf", expert_in, grad_pre_gate, preferred_element_type=jnp.float32
    ).reshape(local_experts, features, units)
    grad_up_w = jnp.einsum(
        "jesd,esf->ejdf", expert_in, grad_pre_up, preferred_element_type=jnp.float32
    ).reshape(local_experts, features, units)
    in_part = jnp.einsum(
        "esf,edf->esd", grad_pre_gate, gate_proj, preferred_element_type=jnp.float32
    )
    in_part = in_part + jnp.einsum(
        "esf,edf->esd", grad_pre_up, up_proj, preferred_element_type=jnp.float32
    )
    out_sum = lax.psum_scatter(out_part.astype(jnp.bfloat16), "et", scatter_dimension=2, tiled=True)
    in_part, grad_gate_w, grad_up_w, grad_down = lax.optimization_barrier(
        (in_part.astype(jnp.bfloat16), grad_gate_w, grad_up_w, grad_down)
    )
    in_sum = lax.psum_scatter(in_part, "et", scatter_dimension=2, tiled=True)
    back_out, back_grad = (
        lax.all_to_all(out_sum, "dp", split_axis=1, concat_axis=0, tiled=True),
        lax.all_to_all(in_sum, "dp", split_axis=1, concat_axis=0, tiled=True),
    )
    back_out = back_out.reshape(slots, width)
    back_grad = back_grad.reshape(slots, width)
    mixed = jnp.einsum(
        "st,sd->td", gate_select, back_out, preferred_element_type=jnp.float32
    ).astype(jnp.bfloat16)
    grad_tokens = jnp.einsum(
        "st,sd->td", select, back_grad, preferred_element_type=jnp.float32
    ).astype(jnp.bfloat16)
    out_rows = (
        back_out[slot_index.reshape(-1)].reshape(tok_rows, per_token, width).astype(jnp.float32)
    )
    gate_part = jnp.sum(cotangent.astype(jnp.float32)[:, None, :] * out_rows, axis=2)
    grad_gates = lax.psum(gate_part, "et")
    return (mixed, grad_tokens, grad_gates, grad_gate_w, grad_up_w, grad_down)


def solution(mesh):
    in_specs = (
        P("dp", "et"),
        P("dp", "et"),
        P("dp", None),
        P("dp", None),
        P("dp", None, "et"),
        P("dp", None, "et"),
        P("dp", "et", None),
    )
    out_specs = (
        P("dp", "et"),
        P("dp", "et"),
        P("dp", None),
        P("dp", None, "et"),
        P("dp", None, "et"),
        P("dp", "et", None),
    )
    return jax.shard_map(local, mesh=mesh, in_specs=in_specs, out_specs=out_specs, check_vma=False)
```

profile of v0, /device:TPU:2, one launch (start us, length us, event | category | flops | bytes accessed | tf_op | source)
XLA Modules:
  0.0 295.2 jit_solution(13721810918180096629)
XLA Ops:
  10.5 33.9 %all_to_all.60 = bf16[64,24,256]{2,1,0:T(8,128)(2,1)S(1)} all-to-all(bf16[64,24,256]{2,1,0:T(8,128)(2,1)S(1)} %bitcast.93), channel_id=1, replica_groups=mesh['dp'=32,'et'=8] {'dp'}, dimensions={0} | all-to-all | bytes 1572864 | tf_op jit(solution)/shard_map/all_to_all | solution.py:50
  47.2 26.7 %all_to_all.61 = bf16[64,24,256]{2,1,0:T(8,128)(2,1)S(1)} all-to-all(bf16[64,24,256]{2,1,0:T(8,128)(2,1)S(1)} %bitcast.94), channel_id=1, replica_groups=mesh['dp'=32,'et'=8] {'dp'}, dimensions={0} | all-to-all | bytes 1572864 | tf_op jit(solution)/shard_map/all_to_all | solution.py:53
  74.9 10.9 %all-gather.3.cloned.1.call-done = bf16[8,2,768,256]{3,2,0,1:T(8,128)(2,1)} async-done(((bf16[1,2,768,256]{3,2,0,1:T(8,128)(2,1)}), bf16[8,2,768,256]{3,2,0,1:T(8,128)(2,1)}) %all-gather.3.cloned.1.call-update) | async-done | bytes 6291472 | tf_op jit(solution)/shard_map/all_gather | solution.py:57
  85.8 5.6 %convolution_bitcast_fusion.1 = f32[2,768,128]{2,1,0:T(8,128)} fusion(bf16[8,2,768,256]{3,2,0,1:T(8,128)(2,1)} %all-gather.3.cloned.1.call-done, bf16[2,8,256,128]{3,2,1,0:T(8,128)(2,1)S(1)} %bitcast.86), kind=kOutput, calls=%fused_computation.16 | convolution fusion | flops 805306368 | bytes 8126464 | tf_op jit(solution)/shard_map/jesd,ejdf->esf/dot_general | solution.py:63
  91.4 2.7 convolution_bitcast_fusion.2
  94.1 37.7 %all-gather.5.cloned.1.call-done = bf16[8,2,768,256]{3,2,0,1:T(8,128)(2,1)} async-done(((bf16[1,2,768,256]{3,2,0,1:T(8,128)(2,1)}), bf16[8,2,768,256]{3,2,0,1:T(8,128)(2,1)}) %all-gather.5.cloned.1.call-update) | async-done | bytes 6291472 | tf_op jit(solution)/shard_map/all_gather | solution.py:58
  131.7 5.7 %multiply_convert_fusion = (bf16[2,768,128]{2,1,0:T(8,128)(2,1)}, bf16[2,768,128]{2,1,0:T(8,128)(2,1)S(1)}, bf16[2,768,128]{2,1,0:T(8,128)(2,1)S(1)}) fusion(f32[2,768,128]{2,1,0:T(8,128)} %convolution_bitcast_fusion.2, f32[2,768,128]{2,1,0:T(8,128)S(1)} %copy-done.11, bf16[8,2,768,256]{3,2,0,1:T(8,128)(2,1)} %all-gather.5.cloned.1.call-done, ...), kind=kOutput, calls=%fused_computation.26 | convolution fusion | flops 808255488 | bytes 10092544 | tf_op jit(solution)/shard_map/jesd,efjd->esf/dot_general | solution.py:68
  138.2 4.4 %convolution_convert_fusion = bf16[2,768,2048]{2,1,0:T(8,128)(2,1)} fusion(bf16[2,768,128]{2,1,0:T(8,128)(2,1)S(1)} %get-tuple-element.34, bf16[2,128,2048]{2,1,0:T(8,128)(2,1)S(1)} %copy-done.10), kind=kOutput, calls=%fused_computation.4 | convolution fusion | flops 808452096 | bytes 7733248 | tf_op jit(solution)/shard_map/esf,efd->esd/dot_general | solution.py:67
  142.9 5.6 %fusion.21 = f32[2,128,8,256]{1,3,2,0:T(8,128)S(1)} fusion(bf16[8,2,768,256]{3,2,0,1:T(8,128)(2,1)} %all-gather.5.cloned.1.call-done, bf16[2,768,128]{2,1,0:T(8,128)(2,1)} %copy-done.9), kind=kOutput, calls=%fused_computation.33 | convolution fusion | flops 805306368 | bytes 8781824 | tf_op jit(solution)/shard_map/esf,jesd->efjd/dot_general | solution.py:75
  148.5 6.8 %fusion.23 = f32[2,8,256,128]{3,2,1,0:T(8,128)} fusion(bf16[8,2,768,256]{3,2,0,1:T(8,128)(2,1)} %all-gather.3.cloned.1.call-done, bf16[2,768,128]{2,1,0:T(8,128)(2,1)} %get-tuple-element.32), kind=kOutput, calls=%fused_computation.35 | convolution fusion | flops 805306368 | bytes 8781824 | tf_op jit(solution)/shard_map/jesd,esf->ejdf/dot_general | solution.py:81
  155.3 4.0 %fusion.25 = f32[2,8,256,128]{3,2,1,0:T(8,128)} fusion(bf16[8,2,768,256]{3,2,0,1:T(8,128)(2,1)S(1)} %bitcast.82, bf16[2,768,128]{2,1,0:T(8,128)(2,1)S(1)} %get-tuple-element.33), kind=kOutput, calls=%fused_computation.37 | convolution fusion | flops 805306368 | bytes 8781824 | tf_op jit(solution)/shard_map/jesd,esf->ejdf/dot_general | solution.py:78
  159.3 1.8 fusion.42
  161.1 4.5 %add_convert_fusion = bf16[2,768,2048]{2,1,0:T(8,128)(2,1)} fusion(f32[2,768,2048]{2,1,0:T(8,128)S(1)} %fusion.42, bf16[2,768,128]{2,1,0:T(8,128)(2,1)S(1)} %copy-done.8, bf16[2,2048,128]{2,1,0:T(8,128)(2,1)S(1)} %copy-done.3), kind=kOutput, calls=%fused_computation.1 | convolution fusion | flops 811597824 | bytes 20316160 | tf_op jit(solution)/shard_map/esf,edf->esd/dot_general | solution.py:87
  165.6 22.3 %reduce-scatter.3.cloned.1.call-done = bf16[2,768,256]{2,1,0:T(8,128)(2,1)} async-done(((bf16[2,768,2048]{2,1,0:T(8,128)(2,1)}), bf16[2,768,256]{2,1,0:T(8,128)(2,1)}) %reduce-scatter.3.cloned.1.call-update) | async-done | bytes 786448 | tf_op jit(solution)/shard_map/reduce_scatter | solution.py:90
  187.9 3.0 %copy.51 = bf16[2,768,256]{2,0,1:T(2,128)(2,1)} copy(bf16[2,768,256]{2,1,0:T(8,128)(2,1)} %reduce-scatter.3.cloned.1.call-done) | data formatting | bytes 1572864 | tf_op jit(solution)/shard_map/reduce_scatter | solution.py:90
  190.9 10.2 %all-to-all-start.1 = ((bf16[2,768,256]{2,0,1:T(2,128)(2,1)}), bf16[2,768,256]{2,0,1:T(2,128)(2,1)}, u32[]{:S(2)}, u32[]{:S(2)}) async-start(bf16[2,768,256]{2,0,1:T(2,128)(2,1)} %copy.51), calls=%async_computation.2 | async-start | bytes 1572864 | tf_op jit(solution)/shard_map/all_to_all | solution.py:96
  201.1 34.5 %reduce-scatter.5.cloned.1.call-done = bf16[2,768,256]{2,1,0:T(8,128)(2,1)} async-done(((bf16[2,768,2048]{2,1,0:T(8,128)(2,1)}), bf16[2,768,256]{2,1,0:T(8,128)(2,1)}) %reduce-scatter.5.cloned.1.call-update) | async-done | bytes 786448 | tf_op jit(solution)/shard_map/reduce_scatter | solution.py:94
  235.7 2.8 copy.59
  238.5 10.3 %all-to-all-start.3 = ((bf16[2,768,256]{2,0,1:T(2,128)(2,1)}), bf16[2,768,256]{2,0,1:T(2,128)(2,1)}, u32[]{:S(2)}, u32[]{:S(2)}) async-start(bf16[2,768,256]{2,0,1:T(2,128)(2,1)} %copy.59), calls=%async_computation.5 | async-start | bytes 1572864 | tf_op jit(solution)/shard_map/all_to_all | solution.py:97
  248.8 1.5 convert_element_type.85
  252.0 1.8 copy.64
  253.8 1.3 copy.52
  255.1 3.9 %gather_fusion = bf16[1024,256]{1,0:T(8,128)(2,1)S(1)} fusion(bf16[1536,256]{1,0:T(8,128)(2,1)S(1)} %bitcast.83, s32[1024]{0:T(1024)S(1)} %broadcast_clamp_fusion), kind=kCustom, calls=%fused_computation | custom fusion | bytes 1052672 | tf_op jit(solution)/shard_map/gather | solution.py:108
  259.3 25.5 %psum.7 = f32[128,8]{1,0:T(8,128)S(1)} all-reduce(f32[128,8]{1,0:T(8,128)S(1)} %fusion.18), channel_id=1, replica_groups=mesh['dp'=32,'et'=8] {'et'}, use_global_device_ids=true, to_apply=%region_4.5 | all-reduce | flops 1024 | bytes 8192 | tf_op jit(solution)/shard_map/psum | solution.py:111
  (75 shorter events, 13.9 us)
Async XLA Ops:
  7.2 84.2 %copy-start = (bf16[2,2048,128]{2,1,0:T(8,128)(2,1)S(1)}, bf16[2,2048,128]{2,1,0:T(8,128)(2,1)}, u32[]{:S(2)}) copy-start(bf16[2,2048,128]{2,1,0:T(8,128)(2,1)} %param.11) | copy-start | bytes 3145732
  7.2 2.9 copy-start.14
  7.2 78.6 %all-gather.3.cloned.1.call-start = ((), (), s32[]{:S(2)}) async-start(), calls=%async_computation.6 | async-start | bytes 7077888 | tf_op jit(solution)/shard_map/all_gather | solution.py:57
  8.2 37.2 %copy-start.16 = (bf16[128,8]{0,1:T(8,128)(2,1)S(1)}, bf16[128,8]{0,1:T(8,128)(2,1)}, u32[]{:S(2)}) copy-start(bf16[128,8]{0,1:T(8,128)(2,1)} %param.10) | copy-start | bytes 6148
  10.1 35.2 %copy-start.4 = (bf16[1536,128]{1,0:T(8,128)(2,1)}, bf16[1536,128]{1,0:T(8,128)(2,1)S(1)}, u32[]{:S(2)}) copy-start(bf16[1536,128]{1,0:T(8,128)(2,1)S(1)} %fusion.11) | copy-start | bytes 1179652
  10.1 36.7 %copy-start.13 = (bf16[128,256]{1,0:T(8,128)(2,1)S(1)}, bf16[128,256]{1,0:T(8,128)(2,1)}, u32[]{:S(2)}) copy-start(bf16[128,256]{1,0:T(8,128)(2,1)} %param.8) | copy-start | bytes 196612
  45.3 40.5 %copy-start.2 = (bf16[2,2048,128]{2,1,0:T(8,128)(2,1)S(1)}, bf16[2,2048,128]{2,1,0:T(8,128)(2,1)}, u32[]{:S(2)}) copy-start(bf16[2,2048,128]{2,1,0:T(8,128)(2,1)} %param.12) | copy-start | bytes 3145732
  45.3 86.4 %all-gather.5.cloned.1.call-start = ((), (), s32[]{:S(2)}) async-start(), calls=%async_computation.8 | async-start | bytes 7077888 | tf_op jit(solution)/shard_map/all_gather | solution.py:58
  46.9 28.0 %copy-start.6 = (bf16[1536,128]{1,0:T(8,128)(2,1)}, bf16[1536,128]{1,0:T(8,128)(2,1)S(1)}, u32[]{:S(2)}) copy-start(bf16[1536,128]{1,0:T(8,128)(2,1)S(1)} %fusion.8) | copy-start | bytes 1179652
  74.9 113.1 %reduce-scatter.3.cloned.1.call-start = ((), (), s32[]{:S(2)}) async-start(), calls=%async_computation.7 | async-start | bytes 7077888 | tf_op jit(solution)/shard_map/reduce_scatter | solution.py:90
  85.8 5.6 %copy-start.1 = (bf16[8,2,768,256]{3,2,0,1:T(8,128)(2,1)S(1)}, bf16[8,2,768,256]{3,2,0,1:T(8,128)(2,1)}, u32[]{:S(2)}) copy-start(bf16[8,2,768,256]{3,2,0,1:T(8,128)(2,1)} %all-gather.3.cloned.1.call-done) | copy-start | bytes 18874372
  85.8 45.9 %copy-start.10 = (bf16[2,128,2048]{2,1,0:T(8,128)(2,1)S(1)}, bf16[2,128,2048]{2,1,0:T(8,128)(2,1)}, u32[]{:S(2)}) copy-start(bf16[2,128,2048]{2,1,0:T(8,128)(2,1)} %param.13) | copy-start | bytes 3145732
  91.4 40.3 %copy-start.11 = (f32[2,768,128]{2,1,0:T(8,128)S(1)}, f32[2,768,128]{2,1,0:T(8,128)}, u32[]{:S(2)}) copy-start(f32[2,768,128]{2,1,0:T(8,128)} %convolution_bitcast_fusion.1) | copy-start | bytes 2359300
  142.6 93.0 %reduce-scatter.5.cloned.1.call-start = ((), (), s32[]{:S(2)}) async-start(), calls=%async_computation.9 | async-start | bytes 7077888 | tf_op jit(solution)/shard_map/reduce_scatter | solution.py:94
  142.8 12.5 %slice-start = ((s8[6291456]{0:T(1024)(128)(4,1)}), s8[4194304]{0:T(1024)(128)(4,1)S(1)}, s32[]{:S(2)}) async-start(s8[6291456]{0:T(1024)(128)(4,1)} %bitcast.81), calls=%async_computation.10 | async-start | bytes 8388608
  148.5 6.8 %slice-start.1 = ((s8[6291456]{0:T(1024)(128)(4,1)}), s8[2097152]{0:T(1024)(128)(4,1)S(1)}, s32[]{:S(2)}) async-start(s8[6291456]{0:T(1024)(128)(4,1)} %bitcast.81), calls=%async_computation.11 | async-start | bytes 4194304
  159.3 1.8 copy-start.3
  159.3 1.8 copy-start.8
  165.6 84.7 %copy-start.15 = (s32[128,8]{0,1:T(8,128)S(1)}, s32[128,8]{0,1:T(8,128)}, u32[]{:S(2)}) copy-start(s32[128,8]{0,1:T(8,128)} %param.9) | copy-start | bytes 12292
  190.9 47.5 %all-to-all-start.1 = ((bf16[2,768,256]{2,0,1:T(2,128)(2,1)}), bf16[2,768,256]{2,0,1:T(2,128)(2,1)}, u32[]{:S(2)}, u32[]{:S(2)}) async-start(bf16[2,768,256]{2,0,1:T(2,128)(2,1)} %copy.51), calls=%async_computation.2 | async-start | bytes 1572864 | tf_op jit(solution)/shard_map/all_to_all | solution.py:96
  238.5 47.0 %copy-start.7 = (bf16[1536,128]{1,0:T(8,128)(2,1)S(1)}, bf16[1536,128]{1,0:T(8,128)(2,1)}, u32[]{:S(2)}) copy-start(bf16[1536,128]{1,0:T(8,128)(2,1)} %copy-done.6) | copy-start | bytes 1179652
  238.5 47.9 %all-to-all-start.3 = ((bf16[2,768,256]{2,0,1:T(2,128)(2,1)}), bf16[2,768,256]{2,0,1:T(2,128)(2,1)}, u32[]{:S(2)}, u32[]{:S(2)}) async-start(bf16[2,768,256]{2,0,1:T(2,128)(2,1)} %copy.59), calls=%async_computation.5 | async-start | bytes 1572864 | tf_op jit(solution)/shard_map/all_to_all | solution.py:97
  253.8 5.3 %copy-start.12 = (f32[128,256]{1,0:T(8,128)S(1)}, f32[128,256]{1,0:T(8,128)}, u32[]{:S(2)}) copy-start(f32[128,256]{1,0:T(8,128)} %convert_element_type.85) | copy-start | bytes 393220
  253.8 33.9 %copy-start.5 = (bf16[1536,128]{1,0:T(8,128)(2,1)S(1)}, bf16[1536,128]{1,0:T(8,128)(2,1)}, u32[]{:S(2)}) copy-start(bf16[1536,128]{1,0:T(8,128)(2,1)} %copy-done.4) | copy-start | bytes 1179652
  (1 other events, 0.7 us)
Sparse Core Ops, SparseCore 0:
  45.4 40.3 all-gather.2
  88.2 43.4 all-gather.4
  142.7 45.1 reduce-scatter.2
  190.3 45.2 reduce-scatter.4
where the time goes:
time: 296 us; the launch traced here: 295 us
  waiting for transfers between devices  105 us (35%)
  blocking collectives  86 us (29%)
  matrix products  46.7 us (16%)
  starting transfers between devices  20.8 us (7%)
  local copies, waits for them, and re-layouts  20.4 us (7%)
  between operations  14.1 us (5%)
    all_gather x1, waiting for transfers between devices, local(): expert_cot = lax.all_gather(expert_cot_part, 'et', axis=0)  37.7 us
    reduce_scatter x1, waiting for transfers between devices, local(): in_sum = lax.psum_scatter(in_part, 'et', scatter_dimension=2, tiled=True)  34.5 us
    all_to_all x1, blocking collectives, local(): lax.all_to_all(picked.reshape(experts, capacity, width), 'dp', split_axis...  33.9 us
    all_to_all x1, blocking collectives, local(): lax.all_to_all(scaled.reshape(experts, capacity, width), 'dp', split_axis...  26.7 us
    psum x1, blocking collectives, local(): grad_gates = lax.psum(gate_part, 'et')  25.5 us
    reduce_scatter x1, waiting for transfers between devices, local(): lax.psum_scatter(out_part.astype(jnp.bfloat16), 'et', scatter_dimension=2...  22.3 us
    all_gather x1, waiting for transfers between devices, local(): expert_in = lax.all_gather(expert_in_part, 'et', axis=0)  10.9 us
    all_to_all x1, starting transfers between devices, local(): lax.all_to_all(in_sum, 'dp', split_axis=1, concat_axis=0, tiled=True)  10.3 us
  transfers between devices with their start and end apart: 6, of which 4 were waited for; matrix products, arithmetic and copies ran while one was open for 17% of the time, Pallas kernels for 0%

commit v1 on v0

--- a/solution.py
+++ b/solution.py
@@ -108,7 +108,7 @@
         back_out[slot_index.reshape(-1)].reshape(tok_rows, per_token, width).astype(jnp.float32)
     )
     gate_part = jnp.sum(cotangent.astype(jnp.float32)[:, None, :] * out_rows, axis=2)
-    grad_gates = lax.psum(gate_part, "et")
+    grad_gates = jnp.sum(jax.lax.all_gather(gate_part, axis_name="et"), axis=0)
     return (mixed, grad_tokens, grad_gates, grad_gate_w, grad_up_w, grad_down)
 
 

time: 296 us -> 284 us (0.959)
  blocking collectives: 86 us -> 73.6 us
    psum x1 -> x0, blocking collectives: 25.5 us -> none  [local(): grad_gates = lax.psum(gate_part, 'et')]
    all_gather x0 -> x1, blocking collectives: none -> 13.1 us  [local(): grad_gates = jnp.sum(jax.lax.all_gather(gate_part, axis_name='et'), axis=0)]
  transfers between devices with their start and end apart: 6 -> 6, of which waited for: 4 -> 4; matrix products, arithmetic and copies ran while one was open for 17% -> 18% of each run, Pallas kernels for 0% -> 0%
where the time goes in v1:
time: 284 us; the launch traced here: 282 us
  waiting for transfers between devices  105 us (37%)
  blocking collectives  73.6 us (26%)
  matrix products  46.7 us (16%)
  starting transfers between devices  20.7 us (7%)
  local copies, waits for them, and re-layouts  19.9 us (7%)
  between operations  14.1 us (5%)
    all_gather x1, waiting for transfers between devices, local(): expert_cot = lax.all_gather(expert_cot_part, 'et', axis=0)  37.7 us
    reduce_scatter x1, waiting for transfers between devices, local(): in_sum = lax.psum_scatter(in_part, 'et', scatter_dimension=2, tiled=True)  34.5 us
    all_to_all x1, blocking collectives, local(): lax.all_to_all(picked.reshape(experts, capacity, width), 'dp', split_axis...  33.9 us
    all_to_all x1, blocking collectives, local(): lax.all_to_all(scaled.reshape(experts, capacity, width), 'dp', split_axis...  26.7 us
    reduce_scatter x1, waiting for transfers between devices, local(): lax.psum_scatter(out_part.astype(jnp.bfloat16), 'et', scatter_dimension=2...  22.3 us
    all_gather x1, blocking collectives, local(): grad_gates = jnp.sum(jax.lax.all_gather(gate_part, axis_name='et'), axis=0)  13.1 us
    all_gather x1, waiting for transfers between devices, local(): expert_in = lax.all_gather(expert_in_part, 'et', axis=0)  10.9 us
    all_to_all x1, starting transfers between devices, local(): lax.all_to_all(out_sum, 'dp', split_axis=1, concat_axis=0, tiled=True)  10.2 us
  transfers between devices with their start and end apart: 6, of which 4 were waited for; matrix products, arithmetic and copies ran while one was open for 18% of the time, Pallas kernels for 0%

profile of v1, /device:TPU:2, one launch (start us, length us, event | category | flops | bytes accessed | tf_op | source)
XLA Modules:
  0.0 282.0 jit_solution(17248986702839260855)
XLA Ops:
  8.8 1.3 fusion.11
  10.5 33.9 %all_to_all.60 = bf16[64,24,256]{2,1,0:T(8,128)(2,1)S(1)} all-to-all(bf16[64,24,256]{2,1,0:T(8,128)(2,1)S(1)} %bitcast.95), channel_id=1, replica_groups=mesh['dp'=32,'et'=8] {'dp'}, dimensions={0} | all-to-all | bytes 1572864 | tf_op jit(solution)/shard_map/all_to_all | solution.py:50
  47.2 26.7 %all_to_all.61 = bf16[64,24,256]{2,1,0:T(8,128)(2,1)S(1)} all-to-all(bf16[64,24,256]{2,1,0:T(8,128)(2,1)S(1)} %bitcast.96), channel_id=1, replica_groups=mesh['dp'=32,'et'=8] {'dp'}, dimensions={0} | all-to-all | bytes 1572864 | tf_op jit(solution)/shard_map/all_to_all | solution.py:53
  74.9 10.9 %all-gather.4.cloned.1.call-done = bf16[8,2,768,256]{3,2,0,1:T(8,128)(2,1)} async-done(((bf16[1,2,768,256]{3,2,0,1:T(8,128)(2,1)}), bf16[8,2,768,256]{3,2,0,1:T(8,128)(2,1)}) %all-gather.4.cloned.1.call-update) | async-done | bytes 6291472 | tf_op jit(solution)/shard_map/all_gather | solution.py:57
  85.8 5.6 %convolution_bitcast_fusion.1 = f32[2,768,128]{2,1,0:T(8,128)} fusion(bf16[8,2,768,256]{3,2,0,1:T(8,128)(2,1)} %all-gather.4.cloned.1.call-done, bf16[2,8,256,128]{3,2,1,0:T(8,128)(2,1)S(1)} %bitcast.88), kind=kOutput, calls=%fused_computation.16 | convolution fusion | flops 805306368 | bytes 8126464 | tf_op jit(solution)/shard_map/jesd,ejdf->esf/dot_general | solution.py:63
  91.4 2.7 convolution_bitcast_fusion.2
  94.1 37.7 %all-gather.6.cloned.1.call-done = bf16[8,2,768,256]{3,2,0,1:T(8,128)(2,1)} async-done(((bf16[1,2,768,256]{3,2,0,1:T(8,128)(2,1)}), bf16[8,2,768,256]{3,2,0,1:T(8,128)(2,1)}) %all-gather.6.cloned.1.call-update) | async-done | bytes 6291472 | tf_op jit(solution)/shard_map/all_gather | solution.py:58
  131.7 5.7 %multiply_convert_fusion = (bf16[2,768,128]{2,1,0:T(8,128)(2,1)}, bf16[2,768,128]{2,1,0:T(8,128)(2,1)S(1)}, bf16[2,768,128]{2,1,0:T(8,128)(2,1)S(1)}) fusion(f32[2,768,128]{2,1,0:T(8,128)} %convolution_bitcast_fusion.2, f32[2,768,128]{2,1,0:T(8,128)S(1)} %copy-done.11, bf16[8,2,768,256]{3,2,0,1:T(8,128)(2,1)} %all-gather.6.cloned.1.call-done, ...), kind=kOutput, calls=%fused_computation.26 | convolution fusion | flops 808255488 | bytes 10092544 | tf_op jit(solution)/shard_map/jesd,efjd->esf/dot_general | solution.py:68
  138.2 4.4 %convolution_convert_fusion = bf16[2,768,2048]{2,1,0:T(8,128)(2,1)} fusion(bf16[2,768,128]{2,1,0:T(8,128)(2,1)S(1)} %get-tuple-element.52, bf16[2,128,2048]{2,1,0:T(8,128)(2,1)S(1)} %copy-done.10), kind=kOutput, calls=%fused_computation.4 | convolution fusion | flops 808452096 | bytes 7733248 | tf_op jit(solution)/shard_map/esf,efd->esd/dot_general | solution.py:67
  142.8 5.6 %fusion.21 = f32[2,128,8,256]{1,3,2,0:T(8,128)S(1)} fusion(bf16[8,2,768,256]{3,2,0,1:T(8,128)(2,1)} %all-gather.6.cloned.1.call-done, bf16[2,768,128]{2,1,0:T(8,128)(2,1)} %copy-done.9), kind=kOutput, calls=%fused_computation.33 | convolution fusion | flops 805306368 | bytes 8781824 | tf_op jit(solution)/shard_map/esf,jesd->efjd/dot_general | solution.py:75
  148.5 6.8 %fusion.23 = f32[2,8,256,128]{3,2,1,0:T(8,128)} fusion(bf16[8,2,768,256]{3,2,0,1:T(8,128)(2,1)} %all-gather.4.cloned.1.call-done, bf16[2,768,128]{2,1,0:T(8,128)(2,1)} %get-tuple-element.50), kind=kOutput, calls=%fused_computation.35 | convolution fusion | flops 805306368 | bytes 8781824 | tf_op jit(solution)/shard_map/jesd,esf->ejdf/dot_general | solution.py:81
  155.3 4.0 %fusion.25 = f32[2,8,256,128]{3,2,1,0:T(8,128)} fusion(bf16[8,2,768,256]{3,2,0,1:T(8,128)(2,1)S(1)} %bitcast.84, bf16[2,768,128]{2,1,0:T(8,128)(2,1)S(1)} %get-tuple-element.51), kind=kOutput, calls=%fused_computation.37 | convolution fusion | flops 805306368 | bytes 8781824 | tf_op jit(solution)/shard_map/jesd,esf->ejdf/dot_general | solution.py:78
  159.3 1.8 fusion.42
  161.1 4.5 %add_convert_fusion = bf16[2,768,2048]{2,1,0:T(8,128)(2,1)} fusion(f32[2,768,2048]{2,1,0:T(8,128)S(1)} %fusion.42, bf16[2,768,128]{2,1,0:T(8,128)(2,1)S(1)} %copy-done.8, bf16[2,2048,128]{2,1,0:T(8,128)(2,1)S(1)} %copy-done.3), kind=kOutput, calls=%fused_computation.1 | convolution fusion | flops 811597824 | bytes 20316160 | tf_op jit(solution)/shard_map/esf,edf->esd/dot_general | solution.py:87
  165.6 22.3 %reduce-scatter.3.cloned.1.call-done = bf16[2,768,256]{2,1,0:T(8,128)(2,1)} async-done(((bf16[2,768,2048]{2,1,0:T(8,128)(2,1)}), bf16[2,768,256]{2,1,0:T(8,128)(2,1)}) %reduce-scatter.3.cloned.1.call-update) | async-done | bytes 786448 | tf_op jit(solution)/shard_map/reduce_scatter | solution.py:90
  187.9 3.0 %copy.98 = bf16[2,768,256]{2,0,1:T(2,128)(2,1)} copy(bf16[2,768,256]{2,1,0:T(8,128)(2,1)} %reduce-scatter.3.cloned.1.call-done) | data formatting | bytes 1572864 | tf_op jit(solution)/shard_map/reduce_scatter | solution.py:90
  190.9 10.2 %all-to-all-start.1 = ((bf16[2,768,256]{2,0,1:T(2,128)(2,1)}), bf16[2,768,256]{2,0,1:T(2,128)(2,1)}, u32[]{:S(2)}, u32[]{:S(2)}) async-start(bf16[2,768,256]{2,0,1:T(2,128)(2,1)} %copy.98), calls=%async_computation.2 | async-start | bytes 1572864 | tf_op jit(solution)/shard_map/all_to_all | solution.py:96
  201.1 34.5 %reduce-scatter.5.cloned.1.call-done = bf16[2,768,256]{2,1,0:T(8,128)(2,1)} async-done(((bf16[2,768,2048]{2,1,0:T(8,128)(2,1)}), bf16[2,768,256]{2,1,0:T(8,128)(2,1)}) %reduce-scatter.5.cloned.1.call-update) | async-done | bytes 786448 | tf_op jit(solution)/shard_map/reduce_scatter | solution.py:94
  235.6 2.8 copy.106
  238.4 10.2 %all-to-all-start.3 = ((bf16[2,768,256]{2,0,1:T(2,128)(2,1)}), bf16[2,768,256]{2,0,1:T(2,128)(2,1)}, u32[]{:S(2)}, u32[]{:S(2)}) async-start(bf16[2,768,256]{2,0,1:T(2,128)(2,1)} %copy.106), calls=%async_computation.5 | async-start | bytes 1572864 | tf_op jit(solution)/shard_map/all_to_all | solution.py:97
  251.0 1.8 copy.111
  252.8 1.3 copy.99
  254.1 3.9 %gather_fusion = bf16[1024,256]{1,0:T(8,128)(2,1)S(1)} fusion(bf16[1536,256]{1,0:T(8,128)(2,1)S(1)} %bitcast.85, s32[1024]{0:T(1024)S(1)} %broadcast_clamp_fusion), kind=kCustom, calls=%fused_computation | custom fusion | bytes 1052672 | tf_op jit(solution)/shard_map/gather | solution.py:108
  258.3 13.1 %all-gather = f32[1024,8]{1,0:T(8,128)S(1)} all-gather(f32[128,8]{1,0:T(8,128)S(1)} %fusion.18), channel_id=2, replica_groups=mesh['dp'=32,'et'=8] {'et'}, dimensions={0}, use_global_device_ids=true | all-gather | bytes 36864 | tf_op jit(solution)/shard_map/all_gather | solution.py:111
  (78 shorter events, 13.4 us)
Async XLA Ops:
  7.2 84.2 %copy-start = (bf16[2,2048,128]{2,1,0:T(8,128)(2,1)S(1)}, bf16[2,2048,128]{2,1,0:T(8,128)(2,1)}, u32[]{:S(2)}) copy-start(bf16[2,2048,128]{2,1,0:T(8,128)(2,1)} %param.11) | copy-start | bytes 3145732
  7.2 2.9 %copy-start.15 = (bf16[128,256]{1,0:T(8,128)(2,1)S(1)}, bf16[128,256]{1,0:T(8,128)(2,1)}, u32[]{:S(2)}) copy-start(bf16[128,256]{1,0:T(8,128)(2,1)} %param.7) | copy-start | bytes 196612
  7.2 78.6 %all-gather.4.cloned.1.call-start = ((), (), s32[]{:S(2)}) async-start(), calls=%async_computation.6 | async-start | bytes 7077888 | tf_op jit(solution)/shard_map/all_gather | solution.py:57
  8.2 37.2 %copy-start.17 = (bf16[128,8]{0,1:T(8,128)(2,1)S(1)}, bf16[128,8]{0,1:T(8,128)(2,1)}, u32[]{:S(2)}) copy-start(bf16[128,8]{0,1:T(8,128)(2,1)} %param.10) | copy-start | bytes 6148
  10.1 35.2 %copy-start.4 = (bf16[1536,128]{1,0:T(8,128)(2,1)}, bf16[1536,128]{1,0:T(8,128)(2,1)S(1)}, u32[]{:S(2)}) copy-start(bf16[1536,128]{1,0:T(8,128)(2,1)S(1)} %fusion.11) | copy-start | bytes 1179652
  10.1 36.7 %copy-start.13 = (bf16[128,256]{1,0:T(8,128)(2,1)S(1)}, bf16[128,256]{1,0:T(8,128)(2,1)}, u32[]{:S(2)}) copy-start(bf16[128,256]{1,0:T(8,128)(2,1)} %param.8) | copy-start | bytes 196612
  45.3 40.5 %copy-start.2 = (bf16[2,2048,128]{2,1,0:T(8,128)(2,1)S(1)}, bf16[2,2048,128]{2,1,0:T(8,128)(2,1)}, u32[]{:S(2)}) copy-start(bf16[2,2048,128]{2,1,0:T(8,128)(2,1)} %param.12) | copy-start | bytes 3145732
  45.3 86.4 %all-gather.6.cloned.1.call-start = ((), (), s32[]{:S(2)}) async-start(), calls=%async_computation.8 | async-start | bytes 7077888 | tf_op jit(solution)/shard_map/all_gather | solution.py:58
  46.9 28.0 %copy-start.6 = (bf16[1536,128]{1,0:T(8,128)(2,1)}, bf16[1536,128]{1,0:T(8,128)(2,1)S(1)}, u32[]{:S(2)}) copy-start(bf16[1536,128]{1,0:T(8,128)(2,1)S(1)} %fusion.8) | copy-start | bytes 1179652
  74.9 113.0 %reduce-scatter.3.cloned.1.call-start = ((), (), s32[]{:S(2)}) async-start(), calls=%async_computation.7 | async-start | bytes 7077888 | tf_op jit(solution)/shard_map/reduce_scatter | solution.py:90
  85.8 5.6 %copy-start.1 = (bf16[8,2,768,256]{3,2,0,1:T(8,128)(2,1)S(1)}, bf16[8,2,768,256]{3,2,0,1:T(8,128)(2,1)}, u32[]{:S(2)}) copy-start(bf16[8,2,768,256]{3,2,0,1:T(8,128)(2,1)} %all-gather.4.cloned.1.call-done) | copy-start | bytes 18874372
  85.8 45.9 %copy-start.10 = (bf16[2,128,2048]{2,1,0:T(8,128)(2,1)S(1)}, bf16[2,128,2048]{2,1,0:T(8,128)(2,1)}, u32[]{:S(2)}) copy-start(bf16[2,128,2048]{2,1,0:T(8,128)(2,1)} %param.13) | copy-start | bytes 3145732
  91.4 40.3 %copy-start.11 = (f32[2,768,128]{2,1,0:T(8,128)S(1)}, f32[2,768,128]{2,1,0:T(8,128)}, u32[]{:S(2)}) copy-start(f32[2,768,128]{2,1,0:T(8,128)} %convolution_bitcast_fusion.1) | copy-start | bytes 2359300
  142.6 93.0 %reduce-scatter.5.cloned.1.call-start = ((), (), s32[]{:S(2)}) async-start(), calls=%async_computation.9 | async-start | bytes 7077888 | tf_op jit(solution)/shard_map/reduce_scatter | solution.py:94
  142.8 12.5 %slice-start = ((s8[6291456]{0:T(1024)(128)(4,1)}), s8[4194304]{0:T(1024)(128)(4,1)S(1)}, s32[]{:S(2)}) async-start(s8[6291456]{0:T(1024)(128)(4,1)} %bitcast.83), calls=%async_computation.10 | async-start | bytes 8388608
  148.5 6.8 %slice-start.1 = ((s8[6291456]{0:T(1024)(128)(4,1)}), s8[2097152]{0:T(1024)(128)(4,1)S(1)}, s32[]{:S(2)}) async-start(s8[6291456]{0:T(1024)(128)(4,1)} %bitcast.83), calls=%async_computation.11 | async-start | bytes 4194304
  159.3 1.8 copy-start.8
  165.6 83.1 %copy-start.14 = (bf16[128,256]{1,0:T(8,128)(2,1)S(1)}, bf16[128,256]{1,0:T(8,128)(2,1)}, u32[]{:S(2)}) copy-start(bf16[128,256]{1,0:T(8,128)(2,1)} %param.8) | copy-start | bytes 196612
  165.6 83.7 %copy-start.16 = (s32[128,8]{0,1:T(8,128)S(1)}, s32[128,8]{0,1:T(8,128)}, u32[]{:S(2)}) copy-start(s32[128,8]{0,1:T(8,128)} %param.9) | copy-start | bytes 12292
  190.9 47.5 %all-to-all-start.1 = ((bf16[2,768,256]{2,0,1:T(2,128)(2,1)}), bf16[2,768,256]{2,0,1:T(2,128)(2,1)}, u32[]{:S(2)}, u32[]{:S(2)}) async-start(bf16[2,768,256]{2,0,1:T(2,128)(2,1)} %copy.98), calls=%async_computation.2 | async-start | bytes 1572864 | tf_op jit(solution)/shard_map/all_to_all | solution.py:96
  238.4 34.7 %all-to-all-start.3 = ((bf16[2,768,256]{2,0,1:T(2,128)(2,1)}), bf16[2,768,256]{2,0,1:T(2,128)(2,1)}, u32[]{:S(2)}, u32[]{:S(2)}) async-start(bf16[2,768,256]{2,0,1:T(2,128)(2,1)} %copy.106), calls=%async_computation.5 | async-start | bytes 1572864 | tf_op jit(solution)/shard_map/all_to_all | solution.py:97
  249.3 22.9 %copy-start.7 = (bf16[1536,128]{1,0:T(8,128)(2,1)S(1)}, bf16[1536,128]{1,0:T(8,128)(2,1)}, u32[]{:S(2)}) copy-start(bf16[1536,128]{1,0:T(8,128)(2,1)} %copy-done.6) | copy-start | bytes 1179652
  252.8 5.3 %copy-start.12 = (f32[128,256]{1,0:T(8,128)S(1)}, f32[128,256]{1,0:T(8,128)}, u32[]{:S(2)}) copy-start(f32[128,256]{1,0:T(8,128)} %convert_element_type.85) | copy-start | bytes 393220
  252.8 21.6 %copy-start.5 = (bf16[1536,128]{1,0:T(8,128)(2,1)S(1)}, bf16[1536,128]{1,0:T(8,128)(2,1)}, u32[]{:S(2)}) copy-start(bf16[1536,128]{1,0:T(8,128)(2,1)} %copy-done.4) | copy-start | bytes 1179652
  (2 other events, 2.6 us)
Sparse Core Ops, SparseCore 0:
  45.4 40.3 all-gather.3
  88.2 43.4 all-gather.5
  142.7 45.1 reduce-scatter.2
  190.3 45.2 reduce-scatter.4
